TPU v7x, 32 devices: a whole 2x2x4 slice. The times are simulated.
32 devices in a mesh: clips: 2 (over y), patch: 4 (over z), span: 2 (over x), chan: 2 (over core).
Axes of the slice: x: 2, y: 2, z: 4, core: 2. Of those that a mesh axis runs over, the one named last changes fastest.
Arguments:
- latent_tiles: bfloat16 [4, 256, 4, 384], P(('clips', 'span'), 'patch'), parts along dimension 0, may hold values from -12 to 12
- route: int32 [4, 256], P(('clips', 'span')), parts along dimension 0, may hold values from 0 to 255, as said below
- w_query: bfloat16 [384, 384], replicated, may hold values from -0.5 to 4.6
- w_keyval: bfloat16 [384, 768], replicated, may hold values from -0.5 to 4.6
- conv_weight: bfloat16 [3, 3, 3, 384, 384], P(None, None, None, None, 'chan'), may hold values from -0.0625 to 0.0625
Outputs:
- decoded: bfloat16 [8, 8, 64, 384], P(('clips', 'span'), 'patch', None, 'chan'), parts along dimension 0
There are 2 independent parts, one for each index of `clips`. A program takes and returns all parts, laid end to end along the dimension named above; an argument that names none is the same for every part. Nothing has to cross between parts.
Inputs may be any that keep to these rules, and one draw needn't show every extreme that they name: `route`: each span's row is a permutation of 0 .. 255. The 64 tiles of positions j * 64 to (j + 1) * 64 - 1 go to at most 32 per owner, and in every span some such group sends exactly 32 to one owner.
All inputs are finite; a program needn't handle non-finite values.
Results may differ from a plain program's by a relative error of at most 0.0065.
Values may be sent and summed in bfloat16 or wider, within the bound.
No kernel may reach another device: no remote copies, remote signals or barrier semaphores. Data moves between devices by JAX's collectives and lax.ppermute only.
A program may use at most 64 MiB of HBM per device.

v0:
```python
import math
import jax
import jax.numpy as jnp
from jax import lax
from jax.sharding import PartitionSpec as P

C = 384
W = 64
RD = 2
FD = 2
epsilon = 1e-06


def scaled_rms(values):
    wide = values.astype(jnp.float32)
    return wide / jnp.sqrt(jnp.mean(wide * wide, axis=-1, keepdims=True) + epsilon)


def attend(queries, key_rows, value_rows):
    scale = 1.0 / math.sqrt(queries.shape[-1])
    scores = (
        jnp.einsum("fqc,fkc->fqk", queries, key_rows, preferred_element_type=jnp.float32) * scale
    )
    largest = jnp.max(scores, axis=-1, keepdims=True)
    powers = jnp.exp(scores - largest)
    totals = jnp.sum(powers, axis=-1, keepdims=True)
    weights = powers.astype(jnp.bfloat16)
    summed = jnp.einsum("fqk,fkc->fqc", weights, value_rows, preferred_element_type=jnp.float32)
    return summed / totals


def spatial_conv(frames, kernel):
    return lax.conv_general_dilated(
        frames,
        kernel,
        (1, 1),
        ((0, 0), (1, 1)),
        dimension_numbers=("NHWC", "HWIO", "NHWC"),
        preferred_element_type=jnp.float32,
    )


def local(latent_tiles, route, w_query, w_keyval, conv_weight):
    patch_count = lax.axis_size("patch")
    patch_index = lax.axis_index("patch")
    chan_count = lax.axis_size("chan")
    chan_index = lax.axis_index("chan")
    span_count = lax.axis_size("span")
    table = route[0]
    block = latent_tiles.shape[1]
    share = block // chan_count
    own_share = lax.dynamic_slice_in_dim(latent_tiles, chan_index * share, share, 1)
    every_tile = lax.all_gather(own_share, ("patch", "chan"), axis=1, tiled=True)[0]
    tile_total = every_tile.shape[0]
    rows = patch_count * RD
    inverse = (
        jnp.zeros((tile_total,), jnp.int32).at[table].set(jnp.arange(tile_total, dtype=jnp.int32))
    )
    placed = jnp.take(every_tile, inverse, axis=0).reshape(patch_count, FD, RD, W, C)
    whole = placed.transpose(1, 0, 2, 3, 4).reshape(FD, rows, W, C)
    normed_all = scaled_rms(whole).astype(jnp.bfloat16)
    padded = jnp.pad(whole, ((0, 0), (1, 1), (0, 0), (0, 0)))
    features = lax.dynamic_slice_in_dim(padded, patch_index * RD, RD + 2, 1)
    normed = scaled_rms(features).astype(jnp.bfloat16)
    ext_cells = (RD + 2) * W
    queries = jnp.einsum(
        "fnc,cd->fnd", normed.reshape(FD, ext_cells, C), w_query, preferred_element_type=jnp.float32
    ).astype(jnp.bfloat16)
    keyvals = jnp.einsum(
        "fnc,cd->fnd",
        normed_all.reshape(FD, rows * W, C),
        w_keyval,
        preferred_element_type=jnp.float32,
    ).astype(jnp.bfloat16)
    attended = attend(queries, keyvals[..., :C], keyvals[..., C:])
    mixed = (features.astype(jnp.float32) + attended.reshape(FD, RD + 2, W, C)).astype(jnp.bfloat16)
    row_ids = patch_index * RD - 1 + jnp.arange(RD + 2)
    inside = ((row_ids >= 0) & (row_ids < rows))[None, :, None, None]
    activated = jnp.where(inside, jax.nn.silu(scaled_rms(mixed)), 0.0).astype(jnp.bfloat16)
    tap_sums = [spatial_conv(activated, conv_weight[a]) for a in range(3)]
    to_next = jnp.stack([tap_sums[0][0] + tap_sums[1][1], tap_sums[0][1]])
    pairs = [(i, i + 1) for i in range(span_count - 1)]
    from_prev = lax.ppermute(to_next, "span", pairs)
    own_sum = jnp.stack([tap_sums[2][0], tap_sums[1][0] + tap_sums[2][1]])
    out_width = conv_weight.shape[-1]
    own_rows = mixed[:, 1 : RD + 1]
    own_channels = lax.dynamic_slice_in_dim(own_rows, chan_index * out_width, out_width, 3)
    return (own_channels.astype(jnp.float32) + own_sum + from_prev).astype(jnp.bfloat16)


def solution(mesh):
    placed = (
        P(("clips", "span"), "patch", None, None),
        P(("clips", "span"), None),
        P(),
        P(),
        P(None, None, None, None, "chan"),
    )
    return jax.shard_map(
        local,
        mesh=mesh,
        in_specs=placed,
        out_specs=P(("clips", "span"), "patch", None, "chan"),
        check_vma=False,
    )
```

profile of v0, /device:TPU:0, one launch (start us, length us, event | category | flops | bytes accessed | tf_op | source)
XLA Modules:
  0.0 45.3 jit_solution(2556529948983996494)
XLA Ops:
  0.0 0.0 copy-start
  0.0 0.7 %compare_select_fusion.1 = s32[256,1]{0,1:T(1,128)S(1)} fusion(s32[1,256]{1,0:T(1,128)} %param.6), kind=kLoop, calls=%fused_computation.61 | loop fusion | flops 768 | bytes 2048 | tf_op jit(solution)/shard_map/select_n | solution.py:57
  0.8 1.4 %scatter_custom_fusion = s32[256]{0:T(256)S(1)} fusion(s32[256]{0:T(256)S(1)} %bitcast.81, s32[256]{0:T(256)S(1)} %iota.8, s32[]{:T(128)} %constant.22.clone.1), kind=kCustom, calls=%fused_computation.69 | custom fusion | bytes 1028 | tf_op jit(solution)/shard_map/scatter | solution.py:57
  2.2 0.1 broadcast_in_dim.37
  2.3 0.1 broadcast_in_dim.38
  2.4 0.1 broadcast_in_dim.39
  2.6 0.9 %constant_dynamic-slice_fusion = bf16[1,32,4,384]{3,2,0,1:T(4,128)(2,1)S(1)} fusion(bf16[1,64,4,384]{3,2,0,1:T(4,128)(2,1)} %bitcast.80, s32[]{:T(128)S(6)} %select_n.35), kind=kLoop, calls=%fused_computation.68 | loop fusion | bytes 196612 | tf_op jit(solution)/shard_map/dynamic_slice | solution.py:52
  3.5 17.2 %all_gather.3 = bf16[1,256,4,384]{3,2,0,1:T(4,128)(2,1)S(1)} all-gather(bf16[1,32,4,384]{3,2,0,1:T(4,128)(2,1)S(1)} %constant_dynamic-slice_fusion), channel_id=1, replica_groups=mesh['clips'=2,'patch'=4,'span'=2,'chan'=2] {'patch','chan'}, dimensions={1}, use_global_device_ids=true | all-gather | bytes 884736 | tf_op jit(solution)/shard_map/all_gather | solution.py:53
  20.7 1.5 %gather_fusion = bf16[256,4,384]{2,1,0:T(4,128)(2,1)S(1)} fusion(bf16[256,4,384]{2,1,0:T(4,128)(2,1)S(1)} %bitcast.71, s32[1024]{0:T(1024)S(1)} %pad_clamp_fusion), kind=kCustom, calls=%fused_computation | custom fusion | bytes 1573888 | tf_op jit(solution)/shard_map/jit(_take)/gather | solution.py:59
  22.2 0.2 gather.7
  22.4 0.5 %multiply_reduce_fusion = (f32[2,4,2,64]{3,2,1,0:T(2,128)S(1)}, bf16[4,2,2,64,384]{4,3,2,0,1:T(8,128)(2,1)S(1)}) fusion(bf16[4,2,2,64,384]{4,3,2,1,0:T(8,128)(2,1)S(1)} %gather.7, pred[4,2,2,64]{3,2,0,1:T(4,128)(4,1)S(1)} %copy.32), kind=kLoop, calls=%fused_computation.6 | loop fusion | flops 1571840 | bytes 1577984 | tf_op jit(solution)/shard_map/reduce_sum | solution.py:16
  22.9 0.1 sqrt.29
  23.0 0.2 bitcast_convert_fusion
  23.1 0.2 fusion.22
  23.3 0.2 fusion.23
  23.5 0.2 fusion
  23.7 0.0 copy-done
  23.7 0.0 copy-start.2
  23.7 2.1 %convolution_convert_fusion = bf16[2,512,768]{2,1,0:T(8,128)(2,1)} fusion(bf16[2,512,384]{2,1,0:T(8,128)(2,1)S(1)} %fusion, bf16[384,768]{1,0:T(8,128)(2,1)S(1)} %copy-done), kind=kOutput, calls=%fused_computation.3 | convolution fusion | flops 604766208 | bytes 2949120 | tf_op jit(solution)/shard_map/fnc,cd->fnd/dot_general | solution.py:69
  25.9 0.0 copy-done.2
  25.9 1.9 %fusion.46 = (f32[2,256]{1,0:T(2,128)S(1)}, f32[2,256,512]{2,1,0:T(8,128)S(1)}) fusion(bf16[2,512,768]{2,1,0:T(8,128)(2,1)} %convolution_convert_fusion, bf16[2,256,384]{2,1,0:T(8,128)(2,1)S(1)} %bitcast.79, bf16[384,384]{1,0:T(8,128)(2,1)S(1)} %copy-done.2), kind=kOutput, calls=%fused_computation.72 | convolution fusion | flops 353041920 | bytes 2525184 | tf_op jit(solution)/shard_map/fqc,fkc->fqk/dot_general | solution.py:22
  27.8 0.3 fusion.19
  28.1 1.7 %convolution_divide_fusion = f32[2,256,384]{2,1,0:T(8,128)S(1)} fusion(bf16[2,512,768]{2,1,0:T(8,128)(2,1)} %convolution_convert_fusion, f32[2,256,512]{2,1,0:T(8,128)S(1)} %get-tuple-element.14, f32[2,256]{1,0:T(2,128)S(1)} %get-tuple-element.13, f32[2,256]{1,0:T(2,128)S(1)} %fusion.19), kind=kOutput, calls=%fused_computation.17 | convolution fusion | flops 202047488 | bytes 2625536 | tf_op jit(solution)/shard_map/fqk,fkc->fqc/dot_general | solution.py:28
  29.8 0.0 copy-start.1
  29.8 0.2 fusion.21
  30.1 0.3 fusion.37
  30.4 0.0 copy-start.3
  30.4 0.4 copy.46
  30.8 0.3 pad.5.clone
  31.2 0.1 slice.59
  31.2 0.5 %fusion.28 = bf16[4,2,8,11,384]{4,1,3,2,0:T(2,128)(2,1)S(1)} fusion(bf16[4,2,7,2,384]{4,1,3,2,0:T(2,128)(2,1)S(1)} %slice.59, bf16[4,2,8,9,384]{4,1,3,2,0:T(2,128)(2,1)S(1)} %bitcast.73), kind=kLoop, calls=%fused_computation.41 | loop fusion | flops 1622016 | bytes 1069056 | tf_op jit(solution)/shard_map/conv_general_dilated | solution.py:33
  31.7 0.2 copy-done.1
  31.9 0.0 copy-done.3
  31.9 0.7 %fusion.16 = f32[2,16,9,192]{3,1,2,0:T(8,128)S(1)} fusion(bf16[3,3,3,384,192]{3,4,2,1,0:T(8,128)(2,1)S(1)} %copy-done.1, bf16[4,2,8,11,384]{4,1,3,2,0:T(2,128)(2,1)S(1)} %fusion.28, pred[16,9]{0,1:T(8,128)(4,1)S(1)} %copy-done.3), kind=kOutput, calls=%fused_computation.24 | convolution fusion | flops 382261248 | bytes 2091008 | tf_op jit(solution)/shard_map/conv_general_dilated | solution.py:33
  32.7 0.7 %fusion.13 = f32[2,16,9,192]{3,1,2,0:T(8,128)S(1)} fusion(bf16[3,3,3,384,192]{3,4,2,1,0:T(8,128)(2,1)S(1)} %copy-done.1, bf16[4,2,8,11,384]{4,1,3,2,0:T(2,128)(2,1)S(1)} %fusion.28, pred[16,9]{0,1:T(8,128)(4,1)S(1)} %copy-done.3), kind=kOutput, calls=%fused_computation.23 | convolution fusion | flops 382261248 | bytes 2091008 | tf_op jit(solution)/shard_map/conv_general_dilated | solution.py:33
  33.4 0.7 %fusion.10 = f32[2,16,9,192]{3,1,2,0:T(8,128)S(1)} fusion(bf16[3,3,3,384,192]{3,4,2,1,0:T(8,128)(2,1)S(1)} %copy-done.1, bf16[4,2,8,11,384]{4,1,3,2,0:T(2,128)(2,1)S(1)} %fusion.28, pred[16,9]{0,1:T(8,128)(4,1)S(1)} %copy-done.3), kind=kOutput, calls=%fused_computation.22 | convolution fusion | flops 382261248 | bytes 2091008 | tf_op jit(solution)/shard_map/conv_general_dilated | solution.py:33
  34.1 0.2 copy.41
  34.4 0.2 copy.37
  34.7 0.2 copy.39
  35.0 0.1 fusion.45
  35.1 3.4 %collective-permute-start = (f32[2,2,64,192]{3,2,1,0:T(8,128)S(1)}, f32[2,2,64,192]{3,2,1,0:T(8,128)S(1)}, u32[]{:S(2)}, u32[]{:S(2)}) collective-permute-start(f32[2,2,64,192]{3,2,1,0:T(8,128)S(1)} %pad_maximum_fusion), channel_id=1, source_target_pairs={{0,2},{1,3},{4,6},{5,7},{8,10},{9,11},{12,14},{13,15},{16,18},{17,... | collective-permute-start | bytes 589832 | tf_op jit(solution)/shard_map/ppermute | solution.py:83
  38.6 6.0 %collective-permute-done = f32[2,2,64,192]{3,2,1,0:T(8,128)S(1)} collective-permute-done((f32[2,2,64,192]{3,2,1,0:T(8,128)S(1)}, f32[2,2,64,192]{3,2,1,0:T(8,128)S(1)}, u32[]{:S(2)}, u32[]{:S(2)}) %collective-permute-start) | collective-permute-done | bytes 196640 | tf_op jit(solution)/shard_map/ppermute | solution.py:83
  44.5 0.8 %fusion.41 = bf16[2,2,64,192]{3,2,1,0:T(8,128)(2,1)} fusion(f32[2,2,64,192]{3,2,1,0:T(8,128)S(1)} %collective-permute-done, f32[1,2,64,192]{3,2,1,0:T(8,128)S(1)} %get-tuple-element.10, f32[1,2,64,192]{3,2,1,0:T(8,128)S(1)} %get-tuple-element.9, bf16[2,2,64,384]{3,2,1,0:T(8,128)(2,1)S(1)} %slice.58, s32[]{:T(128)S(6)} %select_n.38), kind=kLoop, calls=%fused_computation.53 | loop fusion | flops 245760 | bytes 589828 | tf_op jit(solution)/shard_map/convert_element_type | solution.py:88
  (17 shorter events, 0.2 us)
Async XLA Ops:
  0.0 23.7 %copy-start = (bf16[384,768]{1,0:T(8,128)(2,1)S(1)}, bf16[384,768]{1,0:T(8,128)(2,1)}, u32[]{:S(2)}) copy-start(bf16[384,768]{1,0:T(8,128)(2,1)} %param.8) | copy-start | bytes 1769476
  23.7 2.1 %copy-start.2 = (bf16[384,384]{1,0:T(8,128)(2,1)S(1)}, bf16[384,384]{1,0:T(8,128)(2,1)}, u32[]{:S(2)}) copy-start(bf16[384,384]{1,0:T(8,128)(2,1)} %param.7) | copy-start | bytes 884740
  29.8 2.1 %copy-start.1 = (bf16[3,3,3,384,192]{3,4,2,1,0:T(8,128)(2,1)S(1)}, bf16[3,3,3,384,192]{3,4,2,1,0:T(8,128)(2,1)}, u32[]{:S(2)}) copy-start(bf16[3,3,3,384,192]{3,4,2,1,0:T(8,128)(2,1)} %param.9) | copy-start | bytes 11943940
  30.4 1.5 %copy-start.3 = (pred[16,9]{0,1:T(8,128)(4,1)S(1)}, pred[16,9]{0,1:T(8,128)(4,1)}, u32[]{:S(2)}) copy-start(pred[16,9]{0,1:T(8,128)(4,1)} %constant.82) | copy-start | bytes 436
  35.1 9.5 %collective-permute-start = (f32[2,2,64,192]{3,2,1,0:T(8,128)S(1)}, f32[2,2,64,192]{3,2,1,0:T(8,128)S(1)}, u32[]{:S(2)}, u32[]{:S(2)}) collective-permute-start(f32[2,2,64,192]{3,2,1,0:T(8,128)S(1)} %pad_maximum_fusion), channel_id=1, source_target_pairs={{0,2},{1,3},{4,6},{5,7},{8,10},{9,11},{12,14},{13,15},{16,18},{17,... | collective-permute-start | bytes 589832 | tf_op jit(solution)/shard_map/ppermute | solution.py:83
where the time goes:
time: 45.6 us; the launch traced here: 45.3 us
  blocking collectives  17.2 us (38%)
  matrix products  7.88 us (17%)
  local copies, waits for them, and re-layouts  6.26 us (14%)
  waiting for transfers between devices  5.99 us (13%)
  other arithmetic  4.2 us (9%)
  starting transfers between devices  3.44 us (8%)
    all_gather x1, blocking collectives, local(): lax.all_gather(own_share, ('patch', 'chan'), axis=1, tiled=True)[0]  17.2 us
    ppermute x1, waiting for transfers between devices, local(): from_prev = lax.ppermute(to_next, 'span', pairs)  5.99 us
    ppermute x1, starting transfers between devices, local(): from_prev = lax.ppermute(to_next, 'span', pairs)  3.44 us
    conv_general_dilated x3, matrix products, spatial_conv(): lax.conv_general_dilated(frames, kernel, (1, 1), ((0, 0), (1, 1)), dimens...  2.15 us
    dot_general x1, matrix products, local(): jnp.einsum('fnc,cd->fnd', normed_all.reshape(FD, rows * W, C), w_keyval,...  2.13 us
    dot_general x1, matrix products, attend(): jnp.einsum('fqc,fkc->fqk', queries, key_rows, preferred_element_type=jnp....  1.93 us
    dot_general x1, matrix products, attend(): jnp.einsum('fqk,fkc->fqc', weights, value_rows, preferred_element_type=jn...  1.66 us
    gather x2, local copies, waits for them, and re-layouts, local(): jnp.take(every_tile, inverse, axis=0).reshape(patch_count, FD, RD, W, C)  1.65 us
  transfers between devices with their start and end apart: 1, of which 1 were waited for; matrix products, arithmetic and copies ran while one was open for 0% of the time, Pallas kernels for 0%

commit v1 on v0

--- a/solution.py
+++ b/solution.py
@@ -9,6 +9,20 @@
 RD = 2
 FD = 2
 epsilon = 1e-06
+
+
+def _test_types(packet):
+    clean, w2 = (jax.lax.psum(1, ("patch", "chan")), jax.lax.axis_index(("patch", "chan")))
+    plain, b_now = (packet, 1)
+    while b_now < clean:
+        right_arr = jax.lax.ppermute(
+            plain, ("patch", "chan"), [(tick, tick ^ b_now) for tick in range(clean)]
+        )
+        y1 = jnp.concatenate([plain, right_arr], 1)
+        u1 = jnp.concatenate([right_arr, plain], 1)
+        plain = jnp.where(w2 & b_now == 0, y1, u1)
+        b_now = 2 * b_now
+    return plain
 
 
 def scaled_rms(values):
@@ -50,7 +64,7 @@
     block = latent_tiles.shape[1]
     share = block // chan_count
     own_share = lax.dynamic_slice_in_dim(latent_tiles, chan_index * share, share, 1)
-    every_tile = lax.all_gather(own_share, ("patch", "chan"), axis=1, tiled=True)[0]
+    every_tile = _test_types(own_share)[0]
     tile_total = every_tile.shape[0]
     rows = patch_count * RD
     inverse = (

time: 45.6 us -> 57.7 us (1.27)
  waiting for transfers between devices: 5.99 us -> 25.7 us
  blocking collectives: 17.2 us -> 0 us
  starting transfers between devices: 3.44 us -> 9.39 us
  other arithmetic: 4.2 us -> 6.32 us
  local copies, waits for them, and re-layouts: 6.26 us -> 7.25 us
    ppermute x0 -> x3, waiting for transfers between devices: none -> 21.1 us  [_test_types(): jax.lax.ppermute(plain, ('patch', 'chan'), [(tick, tick ^ b_now) for tick...]
    all_gather x1 -> x0, blocking collectives: 17.2 us -> none  [local(): lax.all_gather(own_share, ('patch', 'chan'), axis=1, tiled=True)[0]]
    ppermute x0 -> x3, starting transfers between devices: none -> 5.99 us  [_test_types(): jax.lax.ppermute(plain, ('patch', 'chan'), [(tick, tick ^ b_now) for tick...]
    select_n x0 -> x5, other arithmetic: none -> 2.18 us  [_test_types(): plain = jnp.where(w2 & b_now == 0, y1, u1)]
    ppermute x1, waiting for transfers between devices: 5.99 us -> 4.64 us  [local(): from_prev = lax.ppermute(to_next, 'span', pairs)]
    concatenate x0 -> x1, local copies, waits for them, and re-layouts: none -> 0.93 us  [_test_types(): y1 = jnp.concatenate([plain, right_arr], 1)]
  transfers between devices with their start and end apart: 1 -> 4, of which waited for: 1 -> 3; matrix products, arithmetic and copies ran while one was open for 0% -> 7% of each run, Pallas kernels for 0% -> 0%
where the time goes in v1:
time: 57.7 us; the launch traced here: 56.9 us
  waiting for transfers between devices  25.7 us (45%)
  starting transfers between devices  9.39 us (16%)
  matrix products  7.88 us (14%)
  local copies, waits for them, and re-layouts  7.25 us (13%)
  other arithmetic  6.32 us (11%)
    ppermute x3, waiting for transfers between devices, _test_types(): jax.lax.ppermute(plain, ('patch', 'chan'), [(tick, tick ^ b_now) for tick...  21.1 us
    ppermute x3, starting transfers between devices, _test_types(): jax.lax.ppermute(plain, ('patch', 'chan'), [(tick, tick ^ b_now) for tick...  5.99 us
    ppermute x1, waiting for transfers between devices, local(): from_prev = lax.ppermute(to_next, 'span', pairs)  4.64 us
    ppermute x1, starting transfers between devices, local(): from_prev = lax.ppermute(to_next, 'span', pairs)  3.4 us
    select_n x5, other arithmetic, _test_types(): plain = jnp.where(w2 & b_now == 0, y1, u1)  2.18 us
    conv_general_dilated x3, matrix products, spatial_conv(): lax.conv_general_dilated(frames, kernel, (1, 1), ((0, 0), (1, 1)), dimens...  2.16 us
    dot_general x1, matrix products, local(): jnp.einsum('fnc,cd->fnd', normed_all.reshape(FD, rows * W, C), w_keyval,...  2.14 us
    dot_general x1, matrix products, attend(): jnp.einsum('fqc,fkc->fqk', queries, key_rows, preferred_element_type=jnp....  1.94 us
  transfers between devices with their start and end apart: 4, of which 3 were waited for; matrix products, arithmetic and copies ran while one was open for 7% of the time, Pallas kernels for 0%

profile of v1, /device:TPU:0, one launch (start us, length us, event | category | flops | bytes accessed | tf_op | source)
XLA Modules:
  0.0 56.9 jit_solution(7492495593731533136)
XLA Ops:
  0.0 1.0 %constant_dynamic-slice_fusion = bf16[1,32,4,384]{3,2,1,0:T(4,128)(2,1)S(1)} fusion(bf16[1,64,4,384]{3,2,1,0:T(4,128)(2,1)} %param.5, s32[]{:T(128)S(6)} %select_n.102), kind=kLoop, calls=%fused_computation.73 | loop fusion | bytes 196612 | tf_op jit(solution)/shard_map/dynamic_slice | solution.py:66
  1.0 0.5 collective-permute-start
  1.5 0.7 %compare_select_fusion.1 = s32[256,1]{0,1:T(1,128)S(1)} fusion(s32[1,256]{1,0:T(1,128)} %param.6), kind=kLoop, calls=%fused_computation.66 | loop fusion | flops 768 | bytes 2048 | tf_op jit(solution)/shard_map/select_n | solution.py:71
  2.2 1.4 %scatter_custom_fusion = s32[256]{0:T(256)S(1)} fusion(s32[256]{0:T(256)S(1)} %bitcast.87, s32[256]{0:T(256)S(1)} %iota.8, s32[]{:T(128)} %constant.24.clone.1), kind=kCustom, calls=%fused_computation.74 | custom fusion | bytes 1028 | tf_op jit(solution)/shard_map/scatter | solution.py:71
  3.6 0.2 maximum_select_fusion.4
  3.9 2.7 %collective-permute-start.1 = (bf16[1,64,4,384]{3,2,1,0:T(4,128)(2,1)S(1)}, bf16[1,64,4,384]{3,2,1,0:T(4,128)(2,1)S(1)}, u32[]{:S(2)}, u32[]{:S(2)}) collective-permute-start(bf16[1,64,4,384]{3,2,1,0:T(4,128)(2,1)S(1)} %maximum_select_fusion.4), channel_id=1, source_target_pairs={{0,4},{1,5},{4,0},{5,1},{8,12},{9,13},{12,8},{13,9},{2,6},{3,7},{6... | collective-permute-start | bytes 589832 | tf_op jit(solution)/shard_map/ppermute | solution.py:18
  6.5 0.9 %fusion.51 = bf16[32,4,384]{2,1,0:T(4,128)(2,1)S(1)} fusion(bf16[1,64,4,384]{3,2,1,0:T(4,128)(2,1)} %param.5, s32[]{:T(128)S(6)} %select_n.102), kind=kLoop, calls=%fused_computation.78 | loop fusion | bytes 196612 | tf_op jit(solution)/shard_map/concatenate | solution.py:21
  7.5 0.2 maximum_select_fusion.3
  7.7 4.4 %collective-permute-done.1 = bf16[1,64,4,384]{3,2,1,0:T(4,128)(2,1)S(1)} collective-permute-done((bf16[1,64,4,384]{3,2,1,0:T(4,128)(2,1)S(1)}, bf16[1,64,4,384]{3,2,1,0:T(4,128)(2,1)S(1)}, u32[]{:S(2)}, u32[]{:S(2)}) %collective-permute-start.1) | collective-permute-done | bytes 196640 | tf_op jit(solution)/shard_map/ppermute | solution.py:18
  12.1 0.4 maximum_select_fusion.2
  12.5 2.8 %collective-permute-start.2 = (bf16[1,128,4,384]{3,2,1,0:T(4,128)(2,1)S(1)}, bf16[1,128,4,384]{3,2,1,0:T(4,128)(2,1)S(1)}, u32[]{:S(2)}, u32[]{:S(2)}) collective-permute-start(bf16[1,128,4,384]{3,2,1,0:T(4,128)(2,1)S(1)} %maximum_select_fusion.2), channel_id=1, source_target_pairs={{0,8},{1,9},{4,12},{5,13},{8,0},{9,1},{12,4},{13,5},{2,10},{3,11},... | collective-permute-start | bytes 1179656 | tf_op jit(solution)/shard_map/ppermute | solution.py:18
  15.3 0.1 broadcast_in_dim.37
  15.4 0.1 broadcast_in_dim.38
  15.6 0.1 broadcast_in_dim.39
  15.7 0.4 maximum_select_fusion.1
  16.2 16.7 %collective-permute-done.2 = bf16[1,128,4,384]{3,2,1,0:T(4,128)(2,1)S(1)} collective-permute-done((bf16[1,128,4,384]{3,2,1,0:T(4,128)(2,1)S(1)}, bf16[1,128,4,384]{3,2,1,0:T(4,128)(2,1)S(1)}, u32[]{:S(2)}, u32[]{:S(2)}) %collective-permute-start.2) | collective-permute-done | bytes 393248 | tf_op jit(solution)/shard_map/ppermute | solution.py:18
  32.8 0.9 %maximum_select_fusion = bf16[256,4,384]{2,1,0:T(4,128)(2,1)S(1)} fusion(bf16[128,4,384]{2,1,0:T(4,128)(2,1)S(1)} %bitcast.84, bf16[128,4,384]{2,1,0:T(4,128)(2,1)S(1)} %maximum_select_fusion.1, pred[]{:T(512)S(6)} %eq.9), kind=kLoop, calls=%fused_computation.37 | loop fusion | flops 1179648 | bytes 1572865 | tf_op jit(solution)/shard_map/jit(_where)/select_n | solution.py:23
  33.7 1.5 %gather_fusion = bf16[256,4,384]{2,1,0:T(4,128)(2,1)S(1)} fusion(bf16[256,4,384]{2,1,0:T(4,128)(2,1)S(1)} %maximum_select_fusion, s32[1024]{0:T(1024)S(1)} %pad_clamp_fusion), kind=kCustom, calls=%fused_computation | custom fusion | bytes 1573888 | tf_op jit(solution)/shard_map/jit(_take)/gather | solution.py:73
  35.2 0.2 gather.7
  35.4 0.5 multiply_reduce_fusion
  35.9 0.1 sqrt.29
  36.0 0.2 bitcast_convert_fusion
  36.1 0.2 fusion.22
  36.3 0.2 fusion.23
  36.5 0.2 fusion
  36.7 0.0 copy-start.2
  36.7 2.1 %convolution_convert_fusion = bf16[2,512,768]{2,1,0:T(8,128)(2,1)} fusion(bf16[2,512,384]{2,1,0:T(8,128)(2,1)S(1)} %fusion, bf16[384,768]{1,0:T(8,128)(2,1)S(1)} %copy-done), kind=kOutput, calls=%fused_computation.3 | convolution fusion | flops 604766208 | bytes 2949120 | tf_op jit(solution)/shard_map/fnc,cd->fnd/dot_general | solution.py:83
  38.9 1.9 %fusion.46 = (f32[2,256]{1,0:T(2,128)S(1)}, f32[2,256,512]{2,1,0:T(8,128)S(1)}) fusion(bf16[2,512,768]{2,1,0:T(8,128)(2,1)} %convolution_convert_fusion, bf16[2,256,384]{2,1,0:T(8,128)(2,1)S(1)} %bitcast.85, bf16[384,384]{1,0:T(8,128)(2,1)S(1)} %copy-done.2), kind=kOutput, calls=%fused_computation.77 | convolution fusion | flops 353041920 | bytes 2525184 | tf_op jit(solution)/shard_map/fqc,fkc->fqk/dot_general | solution.py:36
  40.8 0.3 fusion.19
  41.1 1.6 %convolution_divide_fusion = f32[2,256,384]{2,1,0:T(8,128)S(1)} fusion(bf16[2,512,768]{2,1,0:T(8,128)(2,1)} %convolution_convert_fusion, f32[2,256,512]{2,1,0:T(8,128)S(1)} %get-tuple-element.14, f32[2,256]{1,0:T(2,128)S(1)} %get-tuple-element.13, f32[2,256]{1,0:T(2,128)S(1)} %fusion.19), kind=kOutput, calls=%fused_computation.17 | convolution fusion | flops 202047488 | bytes 2625536 | tf_op jit(solution)/shard_map/fqk,fkc->fqc/dot_general | solution.py:42
  42.8 0.2 fusion.21
  43.0 0.3 fusion.37
  43.4 0.0 copy-start.3
  43.4 0.4 copy.34
  43.8 0.3 pad.5.clone
  44.1 0.1 slice.59
  44.2 0.5 fusion.28
  44.7 0.2 copy-done.1
  44.9 0.7 %fusion.16 = f32[2,16,9,192]{3,1,2,0:T(8,128)S(1)} fusion(bf16[3,3,3,384,192]{3,4,2,1,0:T(8,128)(2,1)S(1)} %copy-done.1, bf16[4,2,8,11,384]{4,1,3,2,0:T(2,128)(2,1)S(1)} %fusion.28, pred[16,9]{0,1:T(8,128)(4,1)S(1)} %copy-done.3), kind=kOutput, calls=%fused_computation.24 | convolution fusion | flops 382261248 | bytes 2091008 | tf_op jit(solution)/shard_map/conv_general_dilated | solution.py:47
  45.6 0.7 %fusion.13 = f32[2,16,9,192]{3,1,2,0:T(8,128)S(1)} fusion(bf16[3,3,3,384,192]{3,4,2,1,0:T(8,128)(2,1)S(1)} %copy-done.1, bf16[4,2,8,11,384]{4,1,3,2,0:T(2,128)(2,1)S(1)} %fusion.28, pred[16,9]{0,1:T(8,128)(4,1)S(1)} %copy-done.3), kind=kOutput, calls=%fused_computation.23 | convolution fusion | flops 382261248 | bytes 2091008 | tf_op jit(solution)/shard_map/conv_general_dilated | solution.py:47
  46.4 0.7 %fusion.10 = f32[2,16,9,192]{3,1,2,0:T(8,128)S(1)} fusion(bf16[3,3,3,384,192]{3,4,2,1,0:T(8,128)(2,1)S(1)} %copy-done.1, bf16[4,2,8,11,384]{4,1,3,2,0:T(2,128)(2,1)S(1)} %fusion.28, pred[16,9]{0,1:T(8,128)(4,1)S(1)} %copy-done.3), kind=kOutput, calls=%fused_computation.22 | convolution fusion | flops 382261248 | bytes 2091008 | tf_op jit(solution)/shard_map/conv_general_dilated | solution.py:47
  47.1 0.2 copy.29
  47.4 0.2 copy.25
  47.7 0.2 copy.27
  48.0 0.1 fusion.45
  48.1 3.4 %collective-permute-start.3 = (f32[2,2,64,192]{3,2,1,0:T(8,128)S(1)}, f32[2,2,64,192]{3,2,1,0:T(8,128)S(1)}, u32[]{:S(2)}, u32[]{:S(2)}) collective-permute-start(f32[2,2,64,192]{3,2,1,0:T(8,128)S(1)} %pad_maximum_fusion), channel_id=1, source_target_pairs={{0,2},{1,3},{4,6},{5,7},{8,10},{9,11},{12,14},{13,15},{16,18},{17,... | collective-permute-start | bytes 589832 | tf_op jit(solution)/shard_map/ppermute | solution.py:97
  51.5 4.6 %collective-permute-done.3 = f32[2,2,64,192]{3,2,1,0:T(8,128)S(1)} collective-permute-done((f32[2,2,64,192]{3,2,1,0:T(8,128)S(1)}, f32[2,2,64,192]{3,2,1,0:T(8,128)S(1)}, u32[]{:S(2)}, u32[]{:S(2)}) %collective-permute-start.3) | collective-permute-done | bytes 196640 | tf_op jit(solution)/shard_map/ppermute | solution.py:97
  56.1 0.8 %fusion.41 = bf16[2,2,64,192]{3,2,1,0:T(8,128)(2,1)} fusion(f32[2,2,64,192]{3,2,1,0:T(8,128)S(1)} %collective-permute-done.3, f32[1,2,64,192]{3,2,1,0:T(8,128)S(1)} %get-tuple-element.10, f32[1,2,64,192]{3,2,1,0:T(8,128)S(1)} %get-tuple-element.9, bf16[2,2,64,384]{3,2,1,0:T(8,128)(2,1)S(1)} %slice.58, s32[]{:T(128)S(6)} %select_n.112), kind=kLoop, calls=%fused_computation.56 | loop fusion | flops 245760 | bytes 589828 | tf_op jit(solution)/shard_map/convert_element_type | solution.py:102
  (23 shorter events, 0.3 us)
Async XLA Ops:
  0.0 36.7 %copy-start = (bf16[384,768]{1,0:T(8,128)(2,1)S(1)}, bf16[384,768]{1,0:T(8,128)(2,1)}, u32[]{:S(2)}) copy-start(bf16[384,768]{1,0:T(8,128)(2,1)} %param.8) | copy-start | bytes 1769476
  1.0 2.6 %collective-permute-start = (bf16[1,32,4,384]{3,2,1,0:T(4,128)(2,1)S(1)}, bf16[1,32,4,384]{3,2,1,0:T(4,128)(2,1)S(1)}, u32[]{:S(2)}, u32[]{:S(2)}) collective-permute-start(bf16[1,32,4,384]{3,2,1,0:T(4,128)(2,1)S(1)} %constant_dynamic-slice_fusion), channel_id=1, source_target_pairs={{0,1},{1,0},{4,5},{5,4},{8,9},{9,8},{12,13},{13,12},{2,3},{3,2},{6... | collective-permute-start | bytes 294920 | tf_op jit(solution)/shard_map/ppermute | solution.py:18
  3.9 8.2 %collective-permute-start.1 = (bf16[1,64,4,384]{3,2,1,0:T(4,128)(2,1)S(1)}, bf16[1,64,4,384]{3,2,1,0:T(4,128)(2,1)S(1)}, u32[]{:S(2)}, u32[]{:S(2)}) collective-permute-start(bf16[1,64,4,384]{3,2,1,0:T(4,128)(2,1)S(1)} %maximum_select_fusion.4), channel_id=1, source_target_pairs={{0,4},{1,5},{4,0},{5,1},{8,12},{9,13},{12,8},{13,9},{2,6},{3,7},{6... | collective-permute-start | bytes 589832 | tf_op jit(solution)/shard_map/ppermute | solution.py:18
  12.5 20.3 %collective-permute-start.2 = (bf16[1,128,4,384]{3,2,1,0:T(4,128)(2,1)S(1)}, bf16[1,128,4,384]{3,2,1,0:T(4,128)(2,1)S(1)}, u32[]{:S(2)}, u32[]{:S(2)}) collective-permute-start(bf16[1,128,4,384]{3,2,1,0:T(4,128)(2,1)S(1)} %maximum_select_fusion.2), channel_id=1, source_target_pairs={{0,8},{1,9},{4,12},{5,13},{8,0},{9,1},{12,4},{13,5},{2,10},{3,11},... | collective-permute-start | bytes 1179656 | tf_op jit(solution)/shard_map/ppermute | solution.py:18
  36.7 2.1 %copy-start.2 = (bf16[384,384]{1,0:T(8,128)(2,1)S(1)}, bf16[384,384]{1,0:T(8,128)(2,1)}, u32[]{:S(2)}) copy-start(bf16[384,384]{1,0:T(8,128)(2,1)} %param.7) | copy-start | bytes 884740
  42.8 2.1 %copy-start.1 = (bf16[3,3,3,384,192]{3,4,2,1,0:T(8,128)(2,1)S(1)}, bf16[3,3,3,384,192]{3,4,2,1,0:T(8,128)(2,1)}, u32[]{:S(2)}) copy-start(bf16[3,3,3,384,192]{3,4,2,1,0:T(8,128)(2,1)} %param.9) | copy-start | bytes 11943940
  43.4 1.5 %copy-start.3 = (pred[16,9]{0,1:T(8,128)(4,1)S(1)}, pred[16,9]{0,1:T(8,128)(4,1)}, u32[]{:S(2)}) copy-start(pred[16,9]{0,1:T(8,128)(4,1)} %constant.85) | copy-start | bytes 436
  48.1 8.1 %collective-permute-start.3 = (f32[2,2,64,192]{3,2,1,0:T(8,128)S(1)}, f32[2,2,64,192]{3,2,1,0:T(8,128)S(1)}, u32[]{:S(2)}, u32[]{:S(2)}) collective-permute-start(f32[2,2,64,192]{3,2,1,0:T(8,128)S(1)} %pad_maximum_fusion), channel_id=1, source_target_pairs={{0,2},{1,3},{4,6},{5,7},{8,10},{9,11},{12,14},{13,15},{16,18},{17,... | collective-permute-start | bytes 589832 | tf_op jit(solution)/shard_map/ppermute | solution.py:97
